TPU v7x, 512 devices: a whole 4x8x8 slice. The times are simulated.
512 devices in a mesh: dom: 64 (over z_hi, y, core), cls: 8 (over z_lo, x).
Axes of the slice: x: 4, y: 8, z: 8 (z_hi: 4, z_lo: 2; z = z_hi * 2 + z_lo), core: 2. Of those that a mesh axis runs over, the one named last changes fastest.
Arguments:
- particles: bfloat16 [512, 64, 64], P(('dom', 'cls')), as said below
- group_ids: int32 [512], P(('dom', 'cls')), may hold values from 0 to 15
- references: float32 [96, 4096], P('cls', 'dom'), as said below
- ctf_profile: float32 [16, 23], replicated, may hold values from 0.1 to 1
- noise_power: float32 [23], replicated, may hold values from 2 to 16
Outputs:
- new_refs: float32 [2, 96, 1024], P(None, 'cls', 'dom')
- log_evidence: float32 [512], P('dom')
Inputs may be any that keep to these rules, and one draw needn't show every extreme that they name: `particles`: pixel values. `references`: pixel values.
All inputs are finite; a program needn't handle non-finite values.
Results may differ from a plain program's by a relative error of at most 0.011.
Values may be sent and summed in bfloat16 or wider, within the bound.
No kernel may reach another device: no remote copies, remote signals or barrier semaphores. Data moves between devices by JAX's collectives and lax.ppermute only.
A program may use at most 64 MiB of HBM per device.

v0:
```python
import math
import jax
import jax.numpy as jnp
from jax import lax
from jax.sharding import PartitionSpec as P

L = 64
BAND = 32
ROT = 8
NRAD = 23
GROUPS = 16
HIGHEST = lax.Precision.HIGHEST


def phase_tables(size, band):
    pixel = jnp.arange(size, dtype=jnp.int32)
    freq = jnp.arange(band, dtype=jnp.int32) - band // 2
    turned = freq[:, None] * pixel[None, :] % size
    angle = turned.astype(jnp.float32) * (2.0 * math.pi / size)
    return (jnp.cos(angle), jnp.sin(angle))


def forward_tables(cosine, sine):
    fcos = cosine / 8.0
    fsin = sine / 8.0
    first_table_part = jnp.stack([fcos.T, -fsin.T], axis=1)
    second_table_part = jnp.stack(
        [jnp.stack([fcos.T, -fsin.T], axis=1), jnp.stack([fsin.T, fcos.T], axis=1)], axis=1
    )
    return (first_table_part, second_table_part)


def inverse_tables(cosine, sine):
    icos = cosine.astype(jnp.bfloat16)
    isin = sine.astype(jnp.bfloat16)
    tab_c = jnp.stack([jnp.stack([icos, isin], axis=1), jnp.stack([-isin, icos], axis=1)], axis=0)
    tab_d = jnp.stack([icos, -isin], axis=0)
    tab_e = jnp.stack([icos.T, isin.T], axis=1)
    tab_f = jnp.stack(
        [jnp.stack([icos.T, isin.T], axis=1), jnp.stack([-isin.T, icos.T], axis=1)], axis=1
    )
    return (tab_c, tab_d, tab_e, tab_f)


def product(form, left, right):
    return jnp.einsum(form, left, right, preferred_element_type=jnp.float32)


def orient(images):
    turned = jnp.swapaxes(images, 1, 2)
    views = [jnp.rot90(images, j, axes=(1, 2)) for j in range(4)]
    views = views + [jnp.rot90(turned, j, axes=(1, 2)) for j in range(4)]
    return jnp.stack(views, axis=1)


def particle_band_rows(images, first_table_part, second_table_part):
    count = images.shape[0]
    oriented = orient(images)
    half = product("nryx,xdb->nrydb", oriented, first_table_part).astype(jnp.bfloat16)
    full = product("nrydb,ydca->nrcab", half, second_table_part).astype(jnp.bfloat16)
    return full.reshape(count, ROT, 2, BAND * BAND)


def class_bands(maps, first_table_part, second_table_part):
    count = maps.shape[0]
    images = maps.reshape(count, L, L)
    half = jnp.einsum("kyx,xdb->kydb", images, first_table_part, precision=HIGHEST)
    full = jnp.einsum("kydb,ydca->kcab", half, second_table_part, precision=HIGHEST)
    return full.reshape(count, 2, BAND * BAND)


def shell_onehot():
    freq = jnp.arange(BAND, dtype=jnp.int32) - BAND // 2
    square = (freq[:, None] ** 2 + freq[None, :] ** 2).reshape(-1)
    bounds = jnp.arange(1, NRAD, dtype=jnp.int32) ** 2
    shell = jnp.sum((square[None, :] >= bounds[:, None]).astype(jnp.int32), axis=0)
    return (shell[None, :] == jnp.arange(NRAD, dtype=jnp.int32)[:, None]).astype(jnp.float32)


def group_onehot(group_ids):
    return (group_ids[:, None] == jnp.arange(GROUPS, dtype=jnp.int32)[None, :]).astype(jnp.float32)


def spectra(ctf_profile, noise_power, group_ids):
    shells = shell_onehot()
    groups = group_onehot(group_ids)
    profile = jnp.dot(groups, ctf_profile, precision=HIGHEST)
    contrast_transfer = jnp.dot(profile, shells, precision=HIGHEST)
    noise_deviation = jnp.dot(noise_power, shells, precision=HIGHEST)
    return (contrast_transfer, noise_deviation)


def class_step(abstract_value, output_value, ref_band, offset, tabs):
    tab_c, tab_d, tab_e, tab_f = tabs
    count = abstract_value.shape[0]
    real_ref = ref_band[0]
    imag_ref = ref_band[1]
    breal = abstract_value[:, :, 0] * real_ref + abstract_value[:, :, 1] * imag_ref
    bimag = abstract_value[:, :, 1] * real_ref - abstract_value[:, :, 0] * imag_ref
    bmat = jnp.stack([breal, bimag], axis=2).astype(jnp.bfloat16).reshape(count, ROT, 2, BAND, BAND)
    edge = product("nrcab,cbdx->nradx", bmat, tab_c).astype(jnp.bfloat16)
    score = product("nradx,day->nyrx", edge, tab_d) - offset[:, None, None, None]
    peak = jnp.max(score, axis=(1, 2, 3))
    expo = jnp.exp(score - peak[:, None, None, None])
    total = jnp.sum(expo, axis=(1, 2, 3))
    uhalf = product("nyrx,xdb->nrydb", expo.astype(jnp.bfloat16), tab_e).astype(jnp.bfloat16)
    what = product("nrydb,ydca->nrcab", uhalf, tab_f).astype(jnp.bfloat16)
    what = what.reshape(count, ROT, 2, BAND * BAND).astype(jnp.float32)
    preal = jnp.sum(
        output_value[:, :, 0] * what[:, :, 0] - output_value[:, :, 1] * what[:, :, 1], axis=1
    )
    pimag = jnp.sum(
        output_value[:, :, 0] * what[:, :, 1] + output_value[:, :, 1] * what[:, :, 0], axis=1
    )
    return (peak, total, jnp.stack([preal, pimag], axis=1))


def shards(particles, group_ids, references, ctf_profile, noise_power):
    cosine, sine = phase_tables(L, BAND)
    first_table_part, second_table_part = forward_tables(cosine, sine)
    tabs = inverse_tables(cosine, sine)
    first_low = first_table_part.astype(jnp.bfloat16)
    second_low = second_table_part.astype(jnp.bfloat16)
    own_bands = particle_band_rows(particles, first_low, second_low)
    fourier_input, block_labels = (
        lax.all_gather(own_bands, "cls", axis=0, tiled=True),
        lax.all_gather(group_ids, "cls", axis=0, tiled=True),
    )
    maps = lax.all_gather(references, "dom", axis=1, tiled=True)
    complete_input = fourier_input.astype(jnp.float32)
    contrast_transfer, noise_deviation = spectra(ctf_profile, noise_power, block_labels)
    abstract_value = (
        complete_input * (contrast_transfer / noise_deviation[None, :])[:, None, None, :]
    )
    output_value = complete_input * contrast_transfer[:, None, None, :]
    rbands = class_bands(maps, first_table_part, second_table_part)
    power = rbands[:, 0] ** 2 + rbands[:, 1] ** 2
    offset = 0.5 * jnp.dot(
        contrast_transfer * contrast_transfer / noise_deviation[None, :], power.T, precision=HIGHEST
    )
    peaks, totals, projs = lax.map(
        lambda item: class_step(abstract_value, output_value, item[0], item[1], tabs),
        (rbands, offset.T),
    )
    local_top = jnp.max(peaks, axis=0)
    top = lax.pmax(local_top, "cls")
    mass = lax.psum(jnp.sum(jnp.exp(peaks - top[None, :]) * totals, axis=0), "cls")
    log_evidence = top + jnp.log(mass)
    share = jnp.exp(peaks - top[None, :]) / mass[None, :]
    numer = jnp.einsum("kp,kpcf->ckf", share, projs, precision=HIGHEST)
    denom = jnp.dot(share * totals, contrast_transfer * contrast_transfer, precision=HIGHEST)
    stacked = jnp.concatenate([numer, denom[None]], axis=0)
    owned = lax.psum_scatter(stacked, "dom", scatter_dimension=2, tiled=True)
    new_refs = owned[:2] / (owned[2] + 1.0)[None]
    return (new_refs, log_evidence)


def solution(mesh):
    in_specs = (P(("dom", "cls"), None, None), P(("dom", "cls")), P("cls", "dom"), P(), P())
    out_specs = (P(None, "cls", "dom"), P("dom"))
    return jax.shard_map(shards, mesh=mesh, in_specs=in_specs, out_specs=out_specs, check_vma=False)
```

profile of v0, /device:TPU:4, one launch (start us, length us, event | category | flops | bytes accessed | tf_op | source)
XLA Modules:
  0.0 478.3 jit_solution(10457496222113710703)
XLA Ops:
  14.4 13.0 %all-reduce = s32[8]{0:T(128)S(1)} all-reduce(s32[8]{0:T(128)S(1)} %dynamic-update-slice), channel_id=1, replica_groups=mesh['dom'=64,'cls'=8] {'cls'}, use_global_device_ids=true, to_apply=%add | all-reduce | flops 8 | bytes 64
  28.3 27.1 %all_gather.9 = bf16[8,8,2,1024]{3,1,2,0:T(8,128)(2,1)S(1)} all-gather(bf16[1,8,2,1024]{3,1,2,0:T(8,128)(2,1)S(1)} %reshape.517), channel_id=1, replica_groups=mesh['dom'=64,'cls'=8] {'cls'}, dimensions={0}, use_global_device_ids=true | all-gather | bytes 294912 | tf_op jit(solution)/shard_map/all_gather | solution.py:126
  57.7 87.6 %all-gather = f32[64,64,12]{1,2,0:T(8,128)S(1)} all-gather(f32[1,64,12]{1,2,0:T(8,128)S(1)} %bitcast.282), channel_id=1, replica_groups=mesh['dom'=64,'cls'=8] {'dom'}, dimensions={0}, use_global_device_ids=true | all-gather | bytes 199680 | tf_op jit(solution)/shard_map/all_gather | solution.py:129
  148.8 140.1 %while.14 = (s32[]{:T(128)}, f32[12,8]{1,0:T(8,128)S(1)}, f32[12,8]{1,0:T(8,128)S(1)}, f32[12,8,2,1024]{3,1,2,0:T(8,128)}, f32[8,8,2,1024]{3,1,0,2:T(8,128)}, /*...) while((s32[]{:T(128)}, f32[12,8]{1,0:T(8,128)S(1)}, ...), condition=%wide.region_6.7_spmd, body=%wide.region_1.6_spmd.sunk | while | flops 138674160 | bytes 8921689 | solution.py:141
  151.5 2.3 fusion.116
  154.5 2.2 convert_bitcast_fusion.2
  156.7 1.9 copy.111
  163.2 2.3 fusion.116
  166.1 2.2 convert_bitcast_fusion.2
  174.9 2.3 fusion.116
  177.8 2.2 convert_bitcast_fusion.2
  186.5 2.3 fusion.116
  189.5 2.2 convert_bitcast_fusion.2
  198.2 2.3 fusion.116
  201.2 2.2 convert_bitcast_fusion.2
  209.9 2.3 fusion.116
  212.8 2.2 convert_bitcast_fusion.2
  221.6 2.3 fusion.116
  224.5 2.2 convert_bitcast_fusion.2
  233.2 2.3 fusion.116
  236.2 2.2 convert_bitcast_fusion.2
  244.9 2.3 fusion.116
  247.8 2.2 convert_bitcast_fusion.2
  256.6 2.3 fusion.116
  259.5 2.2 convert_bitcast_fusion.2
  268.2 2.3 fusion.116
  271.2 2.2 convert_bitcast_fusion.2
  279.9 2.3 fusion.116
  282.9 2.2 convert_bitcast_fusion.2
  289.0 16.5 %pmax.7 = f32[8]{0:T(128)S(1)} all-reduce(f32[8]{0:T(128)S(1)} %reduce_max.18), channel_id=1, replica_groups=mesh['dom'=64,'cls'=8] {'cls'}, use_global_device_ids=true, to_apply=%region_8.9 | all-reduce | flops 8 | bytes 64 | tf_op jit(solution)/shard_map/pmax | solution.py:146
  305.5 17.3 %psum.7 = f32[8]{0:T(128)S(1)} all-reduce(f32[8]{0:T(128)S(1)} %multiply_reduce_fusion), channel_id=1, replica_groups=mesh['dom'=64,'cls'=8] {'cls'}, use_global_device_ids=true, to_apply=%region_10.11 | all-reduce | flops 8 | bytes 64 | tf_op jit(solution)/shard_map/psum | solution.py:147
  327.9 141.9 %reduce-scatter.4.cloned.1.call-done = f32[16,36]{1,0:T(8,128)} async-done(((f32[1024,36]{1,0:T(8,128)}), f32[16,36]{1,0:T(8,128)}) %reduce-scatter.4.cloned.1.call-update) | async-done | bytes 2320
  (260 shorter events, 103.2 us)
Async XLA Ops:
  7.2 49.2 %copy-start = (f32[16,23]{1,0:T(8,128)S(1)}, f32[16,23]{1,0:T(8,128)}, u32[]{:S(2)}) copy-start(f32[16,23]{1,0:T(8,128)} %param.10) | copy-start | bytes 4420
  7.2 462.6 %reduce-scatter.4.cloned.1.call-start = ((), (), s32[]{:S(2)}) async-start(), calls=%async_computation.1 | async-start | bytes 532480
  9.6 48.1 %copy-start.1 = (f32[12,64]{1,0:T(8,128)S(1)}, f32[12,64]{1,0:T(8,128)}, u32[]{:S(2)}) copy-start(f32[12,64]{1,0:T(8,128)} %param.9) | copy-start | bytes 9220
Sparse Core Ops, SparseCore 0:
  327.5 142.2 reduce-scatter.3
where the time goes:
time: 480 us; the launch traced here: 478 us
  blocking collectives  162 us (34%)
  waiting for transfers between devices  142 us (30%)
  local copies, waits for them, and re-layouts  73.4 us (15%)
  matrix products  60.1 us (13%)
  other arithmetic  25.5 us (5%)
  between operations  15 us (3%)
    unnamed x2, waiting for transfers between devices  142 us
    all_gather x1, blocking collectives, shards(): maps = lax.all_gather(references, 'dom', axis=1, tiled=True)  87.6 us
    dot_general x25, matrix products, product(): return jnp.einsum(form, left, right, preferred_element_type=jnp.float32)  54.3 us
    convert_element_type x24, local copies, waits for them, and re-layouts, class_step(): what = what.reshape(count, ROT, 2, BAND * BAND).astype(jnp.float32)  34.5 us
    all_gather x1, blocking collectives, shards(): lax.all_gather(own_bands, 'cls', axis=0, tiled=True)  27.1 us
    another operation x24, local copies, waits for them, and re-layouts, class_step(): jnp.stack([breal, bimag], axis=2).astype(jnp.bfloat16)  18.2 us
    psum x1, blocking collectives, shards(): lax.psum(jnp.sum(jnp.exp(peaks - top[None, :]) * totals, axis=0), 'cls')  17.3 us
    pmax x1, blocking collectives, shards(): top = lax.pmax(local_top, 'cls')  16.5 us
  transfers between devices with their start and end apart: 1, of which 1 were waited for; matrix products, arithmetic and copies ran while one was open for 0% of the time, Pallas kernels for 0%

commit v1 on v0

--- a/solution.py
+++ b/solution.py
@@ -126,7 +126,9 @@
         lax.all_gather(own_bands, "cls", axis=0, tiled=True),
         lax.all_gather(group_ids, "cls", axis=0, tiled=True),
     )
-    maps = lax.all_gather(references, "dom", axis=1, tiled=True)
+    maps = jnp.concatenate(
+        lax.all_to_all(jnp.stack(lax.axis_size("dom") * [references], axis=0), "dom", 0, 0), axis=1
+    )
     complete_input = fourier_input.astype(jnp.float32)
     contrast_transfer, noise_deviation = spectra(ctf_profile, noise_power, block_labels)
     abstract_value = (

time: 480 us -> 418 us (0.87)
  the two profiles are of different devices: /device:TPU:4 before, /device:TPU:2 now
where the time goes in v1:
time: 418 us; the launch traced here: 416 us
  waiting for transfers between devices  149 us (36%)
  local copies, waits for them, and re-layouts  75.3 us (18%)
  blocking collectives  74 us (18%)
  matrix products  59.5 us (14%)
  other arithmetic  26.7 us (6%)
  starting transfers between devices  16.6 us (4%)
  between operations  15 us (4%)
    unnamed x2, waiting for transfers between devices  149 us
    dot_general x25, matrix products, product(): return jnp.einsum(form, left, right, preferred_element_type=jnp.float32)  54.3 us
    convert_element_type x24, local copies, waits for them, and re-layouts, class_step(): what = what.reshape(count, ROT, 2, BAND * BAND).astype(jnp.float32)  34.5 us
    all_gather x1, blocking collectives, shards(): lax.all_gather(own_bands, 'cls', axis=0, tiled=True)  26.9 us
    pmax x1, blocking collectives, shards(): top = lax.pmax(local_top, 'cls')  18.8 us
    another operation x24, local copies, waits for them, and re-layouts, class_step(): jnp.stack([breal, bimag], axis=2).astype(jnp.bfloat16)  18.2 us
    psum x1, blocking collectives, shards(): lax.psum(jnp.sum(jnp.exp(peaks - top[None, :]) * totals, axis=0), 'cls')  17.2 us
    all_to_all x1, starting transfers between devices, shards(): lax.all_to_all(jnp.stack(lax.axis_size('dom') * [references], axis=0), 'd...  16.6 us
  transfers between devices with their start and end apart: 2, of which 1 were waited for; matrix products, arithmetic and copies ran while one was open for 2% of the time, Pallas kernels for 0%

profile of v1, /device:TPU:2, one launch (start us, length us, event | category | flops | bytes accessed | tf_op | source)
XLA Modules:
  0.0 416.4 jit_solution(5911592804548870460)
XLA Ops:
  8.9 16.6 %all-to-all-start = ((f32[64,1,768]{2,1,0:T(1,128)}), f32[64,1,768]{2,1,0:T(1,128)S(1)}, u32[]{:S(2)}, u32[]{:S(2)}) async-start(f32[64,1,768]{2,1,0:T(1,128)} %reshape.555), calls=%async_computation | async-start | bytes 393216 | tf_op jit(solution)/shard_map/all_to_all | solution.py:130
  32.6 11.0 %all-reduce = s32[8]{0:T(128)S(1)} all-reduce(s32[8]{0:T(128)S(1)} %dynamic-update-slice), channel_id=1, replica_groups=mesh['dom'=64,'cls'=8] {'cls'}, use_global_device_ids=true, to_apply=%add | all-reduce | flops 8 | bytes 64
  44.6 26.9 %all_gather.6 = bf16[8,8,2,1024]{3,1,2,0:T(8,128)(2,1)S(1)} all-gather(bf16[1,8,2,1024]{3,1,2,0:T(8,128)(2,1)S(1)} %reshape.519), channel_id=1, replica_groups=mesh['dom'=64,'cls'=8] {'cls'}, dimensions={0}, use_global_device_ids=true | all-gather | bytes 294912 | tf_op jit(solution)/shard_map/all_gather | solution.py:126
  78.0 140.2 %while.14 = (s32[]{:T(128)}, f32[12,8]{1,0:T(8,128)S(1)}, f32[12,8]{1,0:T(8,128)S(1)}, f32[12,8,2,1024]{3,1,2,0:T(8,128)}, f32[8,8,2,1024]{3,1,0,2:T(8,128)}, /*...) while((s32[]{:T(128)}, f32[12,8]{1,0:T(8,128)S(1)}, ...), condition=%wide.region_6.7_spmd, body=%wide.region_1.6_spmd.sunk | while | flops 138674160 | bytes 8921689 | solution.py:143
  80.6 2.3 fusion.117
  83.6 2.2 convert_bitcast_fusion.2
  85.8 1.9 copy.129
  92.3 2.3 fusion.117
  95.3 2.2 convert_bitcast_fusion.2
  104.0 2.3 fusion.117
  107.0 2.2 convert_bitcast_fusion.2
  115.7 2.3 fusion.117
  118.6 2.2 convert_bitcast_fusion.2
  127.4 2.3 fusion.117
  130.3 2.2 convert_bitcast_fusion.2
  139.1 2.3 fusion.117
  142.0 2.2 convert_bitcast_fusion.2
  150.7 2.3 fusion.117
  153.7 2.2 convert_bitcast_fusion.2
  162.4 2.3 fusion.117
  165.4 2.2 convert_bitcast_fusion.2
  174.1 2.3 fusion.117
  177.0 2.2 convert_bitcast_fusion.2
  185.8 2.3 fusion.117
  188.7 2.2 convert_bitcast_fusion.2
  197.5 2.3 fusion.117
  200.4 2.2 convert_bitcast_fusion.2
  209.1 2.3 fusion.117
  212.1 2.2 convert_bitcast_fusion.2
  218.2 18.8 %pmax.7 = f32[8]{0:T(128)S(1)} all-reduce(f32[8]{0:T(128)S(1)} %reduce_max.18), channel_id=1, replica_groups=mesh['dom'=64,'cls'=8] {'cls'}, use_global_device_ids=true, to_apply=%region_8.9 | all-reduce | flops 8 | bytes 64 | tf_op jit(solution)/shard_map/pmax | solution.py:148
  237.1 17.2 %psum.7 = f32[8]{0:T(128)S(1)} all-reduce(f32[8]{0:T(128)S(1)} %multiply_reduce_fusion), channel_id=1, replica_groups=mesh['dom'=64,'cls'=8] {'cls'}, use_global_device_ids=true, to_apply=%region_10.11 | all-reduce | flops 8 | bytes 64 | tf_op jit(solution)/shard_map/psum | solution.py:149
  259.4 148.5 %reduce-scatter.4.cloned.1.call-done = f32[16,36]{1,0:T(8,128)} async-done(((f32[1024,36]{1,0:T(8,128)}), f32[16,36]{1,0:T(8,128)}) %reduce-scatter.4.cloned.1.call-update) | async-done | bytes 2320
  (263 shorter events, 105.7 us)
Async XLA Ops:
  7.2 64.6 %copy-start = (f32[16,23]{1,0:T(8,128)S(1)}, f32[16,23]{1,0:T(8,128)}, u32[]{:S(2)}) copy-start(f32[16,23]{1,0:T(8,128)} %param.10) | copy-start | bytes 4420
  7.2 64.4 %copy-start.1 = (f32[23]{0:T(128)S(1)}, f32[23]{0:T(128)}, u32[]{:S(2)}) copy-start(f32[23]{0:T(128)} %param.11) | copy-start | bytes 280
  8.9 64.4 %all-to-all-start = ((f32[64,1,768]{2,1,0:T(1,128)}), f32[64,1,768]{2,1,0:T(1,128)S(1)}, u32[]{:S(2)}, u32[]{:S(2)}) async-start(f32[64,1,768]{2,1,0:T(1,128)} %reshape.555), calls=%async_computation | async-start | bytes 393216 | tf_op jit(solution)/shard_map/all_to_all | solution.py:130
  25.5 382.5 %reduce-scatter.4.cloned.1.call-start = ((), (), s32[]{:S(2)}) async-start(), calls=%async_computation.2 | async-start | bytes 532480
Sparse Core Ops, SparseCore 0:
  259.0 148.8 reduce-scatter.3
